TPU v7x, 32 devices: a whole 2x2x4 slice. The times are simulated.
32 devices in a mesh: grp: 8 (over y, x, core), rep: 4 (over z).
Axes of the slice: x: 2, y: 2, z: 4, core: 2. Of those that a mesh axis runs over, the one named last changes fastest.
Arguments:
- features: bfloat16 [4096, 256], P(('grp', 'rep')), may hold values from -0.0625 to 0.0625
- weight: bfloat16 [256, 256], replicated, may hold values from -0.375 to 0.375
- preact: bfloat16 [4096, 256], P(('grp', 'rep')), may hold values from -6 to 6
- grad_out: bfloat16 [4096, 256], P(('grp', 'rep')), may hold values from -1.5 to 1.5
- degree: int32 [4096], P(('grp', 'rep')), may hold values from 1 to 64
- tile_values: bfloat16 [256, 4, 128, 128], P(('grp', 'rep')), may hold values from 0 to 1
- tile_rows: int32 [256, 4], P(('grp', 'rep')), may hold values from -1 to 3, as said below
Outputs:
- input_grad: float32 [4096, 256], P(('grp', 'rep'))
- weight_grad: float32 [256, 256], replicated
Inputs may be any that keep to these rules, and one draw needn't show every extreme that they name: `tile_rows`: each of the 8 rows of one device (aligned blocks) has up to 4 live slots; in every such block some row has all 4 slots live.
All inputs are finite; a program needn't handle non-finite values.
Results may differ from a plain program's by a relative error of at most 0.013.
Values may be sent and summed in bfloat16 or wider, within the bound.
No kernel may reach another device: no remote copies, remote signals or barrier semaphores. Data moves between devices by JAX's collectives and lax.ppermute only.
A program may use at most 128 MiB of HBM per device.

v0:
```python
import jax
import jax.numpy as jnp
from jax import lax
from jax.sharding import PartitionSpec as P


def tile_masks(tile_rows):
    tile_live = tile_rows >= 0
    clipped = jnp.where(tile_live, tile_rows, 0)
    return (tile_live, clipped)


def per_device(features, weight, preact, grad_out, degree, tile_values, tile_rows):
    rows_here = features.shape[0]
    feature_width = features.shape[1]
    tile_edge = tile_values.shape[2]
    slot_count = tile_values.shape[1]
    row_tiles = lax.axis_size("rep") * rows_here // tile_edge
    inverse = lax.rsqrt(degree.astype(jnp.float32))[:, None]
    grad_pre = jnp.where(preact > 0, grad_out, jnp.zeros_like(grad_out))
    tile_live, clipped = tile_masks(tile_rows)
    scaled = (features.astype(jnp.float32) * inverse).astype(jnp.bfloat16)
    gathered = lax.all_gather(scaled, "grp", axis=0, tiled=True)
    columns = gathered.reshape(-1, tile_edge, feature_width)
    target = jnp.where(tile_live, tile_rows, row_tiles)
    partial_value = jnp.zeros((row_tiles + 1, tile_edge, feature_width), jnp.float32)
    for slot in range(slot_count):
        product = jnp.einsum(
            "cij,cjf->cif", tile_values[:, slot], columns, preferred_element_type=jnp.float32
        )
        partial_value = partial_value.at[target[:, slot]].add(product)
    partial_value = partial_value[:row_tiles]
    summed = lax.psum_scatter(
        partial_value.reshape(row_tiles * tile_edge, feature_width).astype(jnp.bfloat16),
        "rep",
        scatter_dimension=0,
        tiled=True,
    ).astype(jnp.float32)
    aggregated = (summed * inverse).astype(jnp.bfloat16)
    weight_local = lax.dot_general(
        aggregated, grad_pre, (((0,), (0,)), ((), ())), preferred_element_type=jnp.float32
    )
    projected = (
        lax.dot_general(
            grad_pre, weight, (((1,), (1,)), ((), ())), preferred_element_type=jnp.float32
        )
        * inverse
    ).astype(jnp.bfloat16)
    block_rows = lax.all_gather(projected, "rep", axis=0, tiled=True)
    blocks = block_rows.reshape(row_tiles, tile_edge, feature_width)
    picked = jnp.take(blocks, clipped, axis=0)
    picked = jnp.where(tile_live[:, :, None, None], picked, jnp.zeros_like(picked))
    result = jnp.einsum("csij,csif->cjf", tile_values, picked, preferred_element_type=jnp.float32)
    input_grad = (
        lax.psum_scatter(
            result.reshape(rows_here * lax.axis_size("grp"), feature_width),
            "grp",
            scatter_dimension=0,
            tiled=True,
        )
        * inverse
    )
    weight_grad = lax.psum(weight_local, ("grp", "rep"))
    return (input_grad, weight_grad)


def solution(mesh):
    return jax.shard_map(
        per_device,
        mesh=mesh,
        in_specs=(
            P(("grp", "rep"), None),
            P(),
            P(("grp", "rep"), None),
            P(("grp", "rep"), None),
            P(("grp", "rep")),
            P(("grp", "rep"), None, None, None),
            P(("grp", "rep"), None),
        ),
        out_specs=(P(("grp", "rep"), None), P()),
        check_vma=False,
    )
```

profile of v0, /device:TPU:0, one launch (start us, length us, event | category | flops | bytes accessed | tf_op | source)
XLA Modules:
  0.0 254.5 jit_solution(7141739193772190387)
XLA Ops:
  7.2 0.7 broadcast_select_fusion
  7.9 0.7 broadcast_compare_fusion
  8.6 0.7 convert_rsqrt_fusion
  9.3 1.1 fusion.5
  10.4 15.6 %all_gather.6 = bf16[512,256]{1,0:T(8,128)(2,1)S(1)} all-gather(bf16[128,256]{1,0:T(8,128)(2,1)S(1)} %fusion.5), channel_id=1, replica_groups=mesh['grp'=8,'rep'=4] {'rep'}, dimensions={0}, use_global_device_ids=true | all-gather | bytes 327680 | tf_op jit(solution)/shard_map/all_gather | solution.py:49
  26.3 0.7 copy.26
  26.9 0.7 gather_fusion
  28.1 2.4 fusion
  31.1 37.1 %reduce-scatter.3.cloned.1.call-done = f32[128,256]{1,0:T(8,128)} async-done(((f32[1024,256]{1,0:T(8,128)}), f32[128,256]{1,0:T(8,128)}) %reduce-scatter.3.cloned.1.call-update) | async-done | bytes 131088 | tf_op jit(solution)/shard_map/reduce_scatter | solution.py:55
  68.3 1.6 multiply_convert_fusion.1
  69.9 9.8 %all_gather.7 = bf16[1024,256]{1,0:T(8,128)(2,1)S(1)} all-gather(bf16[128,256]{1,0:T(8,128)(2,1)S(1)} %get-tuple-element.10), channel_id=1, replica_groups=mesh['grp'=8,'rep'=4] {'grp'}, dimensions={0}, use_global_device_ids=true | all-gather | bytes 589824 | tf_op jit(solution)/shard_map/all_gather | solution.py:23
  79.7 1.4 convolution_bitcast_fusion.3
  81.8 1.3 convolution_bitcast_fusion
  83.1 2.6 %copy.31 = f32[8,128,256]{2,1,0:T(8,128)} copy(f32[8,128,256]{1,2,0:T(8,128)} %convolution_bitcast_fusion.3) | data formatting | bytes 2097152 | tf_op jit(solution)/shard_map/cij,cjf->cif/dot_general | solution.py:28
  85.6 1.4 copy.34
  87.7 2.5 scatter_fusion
  90.2 2.5 scatter_fusion.1
  92.7 1.3 scatter_fusion.2
  94.0 1.3 scatter_fusion.3
  95.4 0.7 slice.61
  96.2 19.8 %reduce-scatter.5.cloned.1.call-done = bf16[128,256]{1,0:T(8,128)(2,1)} async-done(((bf16[512,256]{1,0:T(8,128)(2,1)}), bf16[128,256]{1,0:T(8,128)(2,1)}) %reduce-scatter.5.cloned.1.call-update) | async-done | bytes 65552 | tf_op jit(solution)/shard_map/reduce_scatter | solution.py:33
  115.9 1.8 fusion.16
  117.8 128.5 %all-reduce.2.cloned.1.call-done = f32[256,256]{1,0:T(8,128)} async-done(((f32[256,256]{1,0:T(8,128)}), f32[256,256]{1,0:T(8,128)}) %all-reduce.2.cloned.1.call-update) | async-done | bytes 262160 | tf_op jit(solution)/shard_map/psum | solution.py:63
  246.3 1.7 copy.56
  (30 shorter events, 2.9 us)
Async XLA Ops:
  7.2 2.1 copy-start
  7.2 61.1 %reduce-scatter.3.cloned.1.call-start = ((), (), s32[]{:S(2)}) async-start(), calls=%async_computation.2 | async-start | bytes 1179648 | tf_op jit(solution)/shard_map/reduce_scatter | solution.py:55
  26.9 1.2 copy-start.1
  28.1 40.1 %copy-start.4 = (bf16[128,256]{1,0:T(8,128)(2,1)S(1)}, bf16[128,256]{1,0:T(8,128)(2,1)}, u32[]{:S(2)}) copy-start(bf16[128,256]{1,0:T(8,128)(2,1)} %param.7) | copy-start | bytes 196612
  30.5 85.4 %reduce-scatter.5.cloned.1.call-start = ((), (), s32[]{:S(2)}) async-start(), calls=%async_computation.3 | async-start | bytes 327680 | tf_op jit(solution)/shard_map/reduce_scatter | solution.py:33
  87.0 0.8 copy-start.6
  87.7 2.5 %copy-start.5 = (s32[8]{0:T(128)S(1)}, s32[8]{0:T(128)}, u32[]{:S(2)}) copy-start(s32[8]{0:T(128)} %get-tuple-element.4) | copy-start | bytes 100
  94.0 21.9 %copy-start.2 = (bf16[128,256]{1,0:T(8,128)(2,1)S(1)}, bf16[128,256]{1,0:T(8,128)(2,1)}, u32[]{:S(2)}) copy-start(bf16[128,256]{1,0:T(8,128)(2,1)} %param.10) | copy-start | bytes 196612
  94.0 21.9 %copy-start.3 = (bf16[128,256]{1,0:T(8,128)(2,1)S(1)}, bf16[128,256]{1,0:T(8,128)(2,1)}, u32[]{:S(2)}) copy-start(bf16[128,256]{1,0:T(8,128)(2,1)} %param.9) | copy-start | bytes 196612
  96.1 150.1 %all-reduce.2.cloned.1.call-start = ((), (), s32[]{:S(2)}) async-start(), calls=%async_computation.4 | async-start | bytes 524288 | tf_op jit(solution)/shard_map/psum | solution.py:63
Sparse Core Ops, SparseCore 0:
  30.7 37.5 reduce-scatter.2
  96.3 19.6 reduce-scatter.4
  122.9 123.2 all-reduce.1
where the time goes:
time: 255 us; the launch traced here: 254 us
  waiting for transfers between devices  185 us (73%)
  blocking collectives  25.4 us (10%)
  between operations  13.9 us (5%)
  other arithmetic  11.8 us (5%)
  local copies, waits for them, and re-layouts  9.19 us (4%)
  matrix products  8.64 us (3%)
    psum x1, waiting for transfers between devices, per_device(): weight_grad = lax.psum(weight_local, ('grp', 'rep'))  128 us
    reduce_scatter x1, waiting for transfers between devices, per_device(): lax.psum_scatter(result.reshape(rows_here * lax.axis_size('grp'), feature...  37.1 us
    reduce_scatter x1, waiting for transfers between devices, per_device(): lax.psum_scatter(partial_value.reshape(row_tiles * tile_edge, feature_wid...  19.8 us
    all_gather x1, blocking collectives, per_device(): block_rows = lax.all_gather(projected, 'rep', axis=0, tiled=True)  15.6 us
    all_gather x1, blocking collectives, per_device(): gathered = lax.all_gather(scaled, 'grp', axis=0, tiled=True)  9.77 us
    scatter-add x4, other arithmetic, per_device(): partial_value = partial_value.at[target[:, slot]].add(product)  7.56 us
  transfers between devices with their start and end apart: 3, of which 3 were waited for; matrix products, arithmetic and copies ran while one was open for 0% of the time, Pallas kernels for 0%

commit v1 on v0

--- a/solution.py
+++ b/solution.py
@@ -20,7 +20,18 @@
     grad_pre = jnp.where(preact > 0, grad_out, jnp.zeros_like(grad_out))
     tile_live, clipped = tile_masks(tile_rows)
     scaled = (features.astype(jnp.float32) * inverse).astype(jnp.bfloat16)
-    gathered = lax.all_gather(scaled, "grp", axis=0, tiled=True)
+    newest, extra, k_now = (lax.axis_size("grp"), lax.axis_index("grp"), scaled.shape[0])
+    field_out, x_next = (scaled, 1)
+    while x_next < newest:
+        field_out = jnp.concatenate(
+            [
+                field_out,
+                lax.ppermute(field_out, "grp", [(j, (j - x_next) % newest) for j in range(newest)]),
+            ],
+            axis=0,
+        )
+        x_next = 2 * x_next
+    gathered = jnp.roll(field_out, extra * k_now, axis=0)
     columns = gathered.reshape(-1, tile_edge, feature_width)
     target = jnp.where(tile_live, tile_rows, row_tiles)
     partial_value = jnp.zeros((row_tiles + 1, tile_edge, feature_width), jnp.float32)

time: 255 us -> 244 us (0.957)
  blocking collectives: 25.4 us -> 14.8 us
  starting transfers between devices: 0.12 us -> 4.94 us
  waiting for transfers between devices: 185 us -> 181 us
    reduce_scatter x1, waiting for transfers between devices: 19.8 us -> 2.76 us  [per_device(): lax.psum_scatter(partial_value.reshape(row_tiles * tile_edge, feature_wid...]
    ppermute x0 -> x3, waiting for transfers between devices: none -> 11.7 us  [per_device(): lax.ppermute(field_out, 'grp', [(j, (j - x_next) % newest) for j in range...]
    all_gather x1 -> x0, blocking collectives: 9.77 us -> none  [per_device(): gathered = lax.all_gather(scaled, 'grp', axis=0, tiled=True)]
    ppermute x0 -> x3, starting transfers between devices: none -> 4.82 us  [per_device(): lax.ppermute(field_out, 'grp', [(j, (j - x_next) % newest) for j in range...]
  transfers between devices with their start and end apart: 3 -> 6, of which waited for: 3 -> 6; matrix products, arithmetic and copies ran while one was open for 0% -> 4% of each run, Pallas kernels for 0% -> 0%
where the time goes in v1:
time: 244 us
  waiting for transfers between devices  181 us (74%)
  blocking collectives  14.8 us (6%)
  between operations  13.9 us (6%)
  other arithmetic  12.2 us (5%)
  local copies, waits for them, and re-layouts  8.74 us (4%)
  matrix products  7.91 us (3%)
  starting transfers between devices  4.94 us (2%)
    psum x1, waiting for transfers between devices, per_device(): weight_grad = lax.psum(weight_local, ('grp', 'rep'))  130 us
    reduce_scatter x1, waiting for transfers between devices, per_device(): lax.psum_scatter(result.reshape(rows_here * lax.axis_size('grp'), feature...  36.6 us
    all_gather x1, blocking collectives, per_device(): block_rows = lax.all_gather(projected, 'rep', axis=0, tiled=True)  14.8 us
    ppermute x3, waiting for transfers between devices, per_device(): lax.ppermute(field_out, 'grp', [(j, (j - x_next) % newest) for j in range...  11.7 us
    scatter-add x4, other arithmetic, per_device(): partial_value = partial_value.at[target[:, slot]].add(product)  7.56 us
  transfers between devices with their start and end apart: 6, of which 6 were waited for; matrix products, arithmetic and copies ran while one was open for 4% of the time, Pallas kernels for 0%

profile of v1, /device:TPU:0, one launch (start us, length us, event | category | flops | bytes accessed | tf_op | source)
XLA Modules:
  0.0 243.9 jit_solution(9214949316030021556)
XLA Ops:
  7.9 0.9 constant_dynamic-update-slice_fusion.7
  8.9 3.4 %collective-permute-start = (bf16[128,256]{1,0:T(8,128)(2,1)S(1)}, bf16[128,256]{1,0:T(8,128)(2,1)S(1)}, u32[]{:S(2)}, u32[]{:S(2)}) collective-permute-start(bf16[128,256]{1,0:T(8,128)(2,1)S(1)} %get-tuple-element.3), channel_id=1, source_target_pairs={{0,28},{4,0},{8,4},{12,8},{16,12},{20,16},{24,20},{28,24},{1,29},{... | collective-permute-start | bytes 196616 | tf_op jit(solution)/shard_map/ppermute | solution.py:29
  12.2 1.1 fusion.5
  13.3 0.7 broadcast_select_fusion
  14.8 5.2 %collective-permute-done.1 = bf16[256,256]{1,0:T(8,128)(2,1)S(1)} collective-permute-done((bf16[256,256]{1,0:T(8,128)(2,1)S(1)}, bf16[256,256]{1,0:T(8,128)(2,1)S(1)}, u32[]{:S(2)}, u32[]{:S(2)}) %collective-permute-start.1) | collective-permute-done | bytes 131104 | tf_op jit(solution)/shard_map/ppermute | solution.py:29
  20.0 0.8 collective-permute-start.2
  21.6 6.3 %collective-permute-done.2 = bf16[512,256]{1,0:T(8,128)(2,1)S(1)} collective-permute-done((bf16[512,256]{1,0:T(8,128)(2,1)S(1)}, bf16[512,256]{1,0:T(8,128)(2,1)S(1)}, u32[]{:S(2)}, u32[]{:S(2)}) %collective-permute-start.2) | collective-permute-done | bytes 262176 | tf_op jit(solution)/shard_map/ppermute | solution.py:29
  28.0 1.4 convolution_bitcast_fusion.3
  30.1 1.3 convolution_bitcast_fusion
  31.4 2.5 %copy.27 = f32[8,128,256]{2,1,0:T(8,128)} copy(f32[8,128,256]{1,2,0:T(8,128)} %convolution_bitcast_fusion.3) | data formatting | bytes 2097152 | tf_op jit(solution)/shard_map/cij,cjf->cif/dot_general | solution.py:39
  34.0 1.4 copy.30
  36.1 2.5 %scatter_fusion = f32[5,128,256]{2,1,0:T(8,128)S(1)} fusion(f32[5,128,256]{2,1,0:T(8,128)S(1)} %broadcast_in_dim.40, s32[8]{0:T(128)S(1)} %get-tuple-element.7, f32[8,128,256]{2,1,0:T(8,128)} %copy.27), kind=kCustom, calls=%fused_computation.1 | custom fusion | flops 262144 | bytes 3145760 | tf_op jit(solution)/shard_map/scatter-add | solution.py:42
  38.6 2.5 %scatter_fusion.1 = f32[5,128,256]{2,1,0:T(8,128)S(1)} fusion(f32[5,128,256]{2,1,0:T(8,128)S(1)} %scatter_fusion, s32[8]{0:T(128)S(1)} %get-tuple-element.6, f32[8,128,256]{2,1,0:T(8,128)} %copy.30), kind=kCustom, calls=%fused_computation.2 | custom fusion | flops 262144 | bytes 3145760 | tf_op jit(solution)/shard_map/scatter-add | solution.py:42
  41.0 1.3 scatter_fusion.2
  42.4 1.3 scatter_fusion.3
  43.7 0.7 slice.61
  44.5 14.8 %all_gather.3 = bf16[512,256]{1,0:T(8,128)(2,1)S(1)} all-gather(bf16[128,256]{1,0:T(8,128)(2,1)S(1)} %fusion.5), channel_id=1, replica_groups=mesh['grp'=8,'rep'=4] {'rep'}, dimensions={0}, use_global_device_ids=true | all-gather | bytes 327680 | tf_op jit(solution)/shard_map/all_gather | solution.py:60
  60.9 1.6 fusion
  62.6 2.8 %reduce-scatter.5.cloned.1.call-done = bf16[128,256]{1,0:T(8,128)(2,1)} async-done(((bf16[512,256]{1,0:T(8,128)(2,1)}), bf16[128,256]{1,0:T(8,128)(2,1)}) %reduce-scatter.5.cloned.1.call-update) | async-done | bytes 65552 | tf_op jit(solution)/shard_map/reduce_scatter | solution.py:44
  65.3 1.8 fusion.16
  67.2 36.6 %reduce-scatter.3.cloned.1.call-done = f32[128,256]{1,0:T(8,128)} async-done(((f32[1024,256]{1,0:T(8,128)}), f32[128,256]{1,0:T(8,128)}) %reduce-scatter.3.cloned.1.call-update) | async-done | bytes 131088 | tf_op jit(solution)/shard_map/reduce_scatter | solution.py:66
  103.7 1.6 broadcast_multiply_fusion
  105.4 130.3 %all-reduce.2.cloned.1.call-done = f32[256,256]{1,0:T(8,128)} async-done(((f32[256,256]{1,0:T(8,128)}), f32[256,256]{1,0:T(8,128)}) %all-reduce.2.cloned.1.call-update) | async-done | bytes 262160 | tf_op jit(solution)/shard_map/psum | solution.py:74
  235.7 1.7 copy.59
  (42 shorter events, 5.5 us)
Async XLA Ops:
  7.2 5.1 %copy-start = (bf16[256,256]{1,0:T(8,128)(2,1)S(1)}, bf16[256,256]{1,0:T(8,128)(2,1)}, u32[]{:S(2)}) copy-start(bf16[256,256]{1,0:T(8,128)(2,1)} %param.8) | copy-start | bytes 393220
  7.2 58.2 %reduce-scatter.5.cloned.1.call-start = ((), (), s32[]{:S(2)}) async-start(), calls=%async_computation.3 | async-start | bytes 327680 | tf_op jit(solution)/shard_map/reduce_scatter | solution.py:44
  8.8 19.2 %copy-start.1 = (bf16[8,4,128,128]{3,2,1,0:T(8,128)(2,1)S(1)}, bf16[8,4,128,128]{3,2,1,0:T(8,128)(2,1)}, u32[]{:S(2)}) copy-start(bf16[8,4,128,128]{3,2,1,0:T(8,128)(2,1)} %param.12) | copy-start | bytes 3145732
  8.9 5.3 %collective-permute-start = (bf16[128,256]{1,0:T(8,128)(2,1)S(1)}, bf16[128,256]{1,0:T(8,128)(2,1)S(1)}, u32[]{:S(2)}, u32[]{:S(2)}) collective-permute-start(bf16[128,256]{1,0:T(8,128)(2,1)S(1)} %get-tuple-element.3), channel_id=1, source_target_pairs={{0,28},{4,0},{8,4},{12,8},{16,12},{20,16},{24,20},{28,24},{1,29},{... | collective-permute-start | bytes 196616 | tf_op jit(solution)/shard_map/ppermute | solution.py:29
  14.2 5.8 %collective-permute-start.1 = (bf16[256,256]{1,0:T(8,128)(2,1)S(1)}, bf16[256,256]{1,0:T(8,128)(2,1)S(1)}, u32[]{:S(2)}, u32[]{:S(2)}) collective-permute-start(bf16[256,256]{1,0:T(8,128)(2,1)S(1)} %pad_maximum_fusion.1), channel_id=1, source_target_pairs={{0,24},{4,28},{8,0},{12,4},{16,8},{20,12},{24,16},{28,20},{1,25},{... | collective-permute-start | bytes 393224 | tf_op jit(solution)/shard_map/ppermute | solution.py:29
  20.0 7.9 %collective-permute-start.2 = (bf16[512,256]{1,0:T(8,128)(2,1)S(1)}, bf16[512,256]{1,0:T(8,128)(2,1)S(1)}, u32[]{:S(2)}, u32[]{:S(2)}) collective-permute-start(bf16[512,256]{1,0:T(8,128)(2,1)S(1)} %pad_maximum_fusion), channel_id=1, source_target_pairs={{0,16},{4,20},{8,24},{12,28},{16,0},{20,4},{24,8},{28,12},{1,17},{... | collective-permute-start | bytes 786440 | tf_op jit(solution)/shard_map/ppermute | solution.py:29
  44.4 59.3 %reduce-scatter.3.cloned.1.call-start = ((), (), s32[]{:S(2)}) async-start(), calls=%async_computation.2 | async-start | bytes 1179648 | tf_op jit(solution)/shard_map/reduce_scatter | solution.py:66
  59.6 1.2 copy-start.2
  60.9 4.5 %copy-start.3 = (bf16[128,256]{1,0:T(8,128)(2,1)S(1)}, bf16[128,256]{1,0:T(8,128)(2,1)}, u32[]{:S(2)}) copy-start(bf16[128,256]{1,0:T(8,128)(2,1)} %param.10) | copy-start | bytes 196612
  60.9 4.5 %copy-start.4 = (bf16[128,256]{1,0:T(8,128)(2,1)S(1)}, bf16[128,256]{1,0:T(8,128)(2,1)}, u32[]{:S(2)}) copy-start(bf16[128,256]{1,0:T(8,128)(2,1)} %param.9) | copy-start | bytes 196612
  62.5 173.2 %all-reduce.2.cloned.1.call-start = ((), (), s32[]{:S(2)}) async-start(), calls=%async_computation.4 | async-start | bytes 524288 | tf_op jit(solution)/shard_map/psum | solution.py:74
Sparse Core Ops, SparseCore 0:
  44.6 20.7 reduce-scatter.4
  68.8 34.8 reduce-scatter.2
  110.7 124.9 all-reduce.1
